TPU v7x, 256 devices: a whole 4x4x8 slice. The times are simulated.
256 devices in a mesh: dp: 8 (over y, core), seq: 32 (over x, z).
Axes of the slice: x: 4, y: 4, z: 8, core: 2. Of those that a mesh axis runs over, the one named last changes fastest.
Arguments:
- queries: bfloat16 [16, 2048, 1536], P('dp', 'seq'), may hold values from -6 to 6
- key_rows: bfloat16 [16, 2048, 1536], P('dp', 'seq'), may hold values from -6 to 6
- value_rows: bfloat16 [16, 2048, 1536], P('dp', 'seq'), may hold values from -6 to 6
- layer_input: bfloat16 [16, 2048, 1536], P('dp', 'seq'), may hold values from -6 to 6
- utt_lengths: int32 [16], P('dp'), may hold values from 512 to 2048, as said below
- out_weight: bfloat16 [1536, 1536], replicated, may hold values from -0.15625 to 0.15625
- conv_kernel: bfloat16 [31, 1536], replicated, may hold values from -1 to 1
- conv_cotangent: bfloat16 [16, 2048, 1536], P('dp', 'seq'), may hold values from -6 to 6
- pick_weight: int32 [23592], replicated, may hold values from 0 to 2359295
- pick_kernel: int32 [476], replicated, may hold values from 0 to 47615
Outputs:
- conv_out: bfloat16 [16, 2048, 1536], P('dp', 'seq')
- context_grad: bfloat16 [16, 2048, 1536], P('dp', 'seq')
- weight_picks: float32 [23592], replicated
- kernel_picks: float32 [476], replicated
Inputs may be any that keep to these rules, and one draw needn't show every extreme that they name: `utt_lengths`: the first utterance fills all 2048 slots and the last has 512 valid frames.
All inputs are finite; a program needn't handle non-finite values.
Results may differ from a plain program's by a relative error of at most 0.0056.
Values may be sent and summed in bfloat16 or wider, within the bound.
No kernel may reach another device: no remote copies, remote signals or barrier semaphores. Data moves between devices by JAX's collectives and lax.ppermute only.
A program may use at most 128 MiB of HBM per device.

v0:
```python
import math
import jax
import jax.numpy as jnp
from jax import lax
from jax.sharding import PartitionSpec as P

HEADS = 16
neg_big = -1e30


def padded(value, sides, width):
    for axis, dim in sides:
        count, length = (lax.axis_size(axis), value.shape[dim])
        up = [(i, (i + 1) % count) for i in range(count - 1)]
        down = [(j, i) for i, j in up]
        last = lax.slice_in_dim(value, length - width, length, axis=dim)
        leading = lax.slice_in_dim(value, 0, width, axis=dim)
        before = lax.ppermute(last, axis, up)
        after = lax.ppermute(leading, axis, down)
        value = jnp.concatenate([before, value, after], axis=dim)
    return value


def softmax_rows(scores, key_ok):
    scores = jnp.where(key_ok, scores, neg_big)
    row_max = jnp.max(scores, axis=-1, keepdims=True)
    probs = jnp.exp(scores - row_max)
    return (probs.astype(jnp.bfloat16), jnp.sum(probs, axis=-1))


def pick_entries(table, picks):
    flat = table.reshape(-1)
    lane = math.gcd(flat.shape[0], 128)
    blocks = flat.reshape(flat.shape[0] // lane, lane)
    chosen = jnp.take(blocks, picks // lane, axis=0)
    lane_ids = jnp.arange(lane, dtype=jnp.int32)
    hit = lane_ids[None, :] == (picks % lane)[:, None]
    return jnp.sum(jnp.where(hit, chosen, jnp.float32(0.0)), axis=1)


def on_device(
    queries,
    key_rows,
    value_rows,
    layer_input,
    utt_lengths,
    out_weight,
    conv_kernel,
    conv_cotangent,
    pick_weight,
    pick_kernel,
):
    local_utts, frames_dev, width = queries.shape
    seq_count = lax.axis_size("seq")
    full_frames = frames_dev * seq_count
    head_size = width // HEADS
    score_scale = 1.0 / math.sqrt(head_size)
    first_frame = lax.axis_index("seq") * frames_dev
    local_ids = first_frame + jnp.arange(frames_dev, dtype=jnp.int32)
    valid_rows = (local_ids[None, :] < utt_lengths[:, None]).astype(jnp.float32)
    all_keys, all_values = (
        lax.all_gather(key_rows, "seq", axis=1, tiled=True),
        lax.all_gather(value_rows, "seq", axis=1, tiled=True),
    )
    full_ids = jnp.arange(full_frames, dtype=jnp.int32)

    def one_utt(item):
        query_utt, key_utt, value_utt, length_utt = item
        query_heads = query_utt.reshape(frames_dev, HEADS, head_size)
        key_heads = key_utt.reshape(full_frames, HEADS, head_size)
        value_heads = value_utt.reshape(full_frames, HEADS, head_size)
        scores = (
            jnp.einsum("qhd,khd->hqk", query_heads, key_heads, preferred_element_type=jnp.float32)
            * score_scale
        )
        weights, denom = softmax_rows(scores, (full_ids < length_utt)[None, None, :])
        out_rows = jnp.einsum(
            "hqk,khd->qhd", weights, value_heads, preferred_element_type=jnp.float32
        )
        out_rows = out_rows / denom.transpose(1, 0)[:, :, None]
        return out_rows.astype(jnp.bfloat16).reshape(frames_dev, width)

    context = lax.map(one_utt, (queries, all_keys, all_values, utt_lengths))
    context_flat = context.reshape(local_utts * frames_dev, width)
    projected = jnp.dot(context_flat, out_weight, preferred_element_type=jnp.float32).reshape(
        local_utts, frames_dev, width
    )
    hidden = ((layer_input.astype(jnp.float32) + projected) * valid_rows[:, :, None]).astype(
        jnp.bfloat16
    )
    tap_count = conv_kernel.shape[0]
    half_taps = (tap_count - 1) // 2
    kernel_f = conv_kernel.astype(jnp.float32)
    hidden_pad = padded(hidden, (("seq", 1),), half_taps)
    cot_f = conv_cotangent.astype(jnp.float32)
    conv_sum = jnp.zeros((local_utts, frames_dev, width), jnp.float32)
    kernel_rows = []
    for offset in range(tap_count):
        window = hidden_pad[:, offset : offset + frames_dev].astype(jnp.float32)
        conv_sum = conv_sum + kernel_f[offset] * window
        kernel_rows.append(jnp.sum(window * cot_f, axis=(0, 1)))
    conv_out = conv_sum.astype(jnp.bfloat16)
    kernel_grad = jnp.stack(kernel_rows)
    cot_pad = padded(conv_cotangent, (("seq", 1),), half_taps).astype(jnp.float32)
    back_sum = jnp.zeros((local_utts, frames_dev, width), jnp.float32)
    for offset in range(tap_count):
        begin = 2 * half_taps - offset
        back_sum = back_sum + kernel_f[offset] * cot_pad[:, begin : begin + frames_dev]
    hidden_grad = (back_sum * valid_rows[:, :, None]).astype(jnp.bfloat16)
    grad_flat = hidden_grad.reshape(local_utts * frames_dev, width)
    weight_grad = lax.dot_general(
        context_flat, grad_flat, (((0,), (0,)), ((), ())), preferred_element_type=jnp.float32
    )
    context_grad = lax.dot_general(
        grad_flat, out_weight, (((1,), (1,)), ((), ())), preferred_element_type=jnp.float32
    )
    context_grad = context_grad.reshape(local_utts, frames_dev, width).astype(jnp.bfloat16)
    weight_vals = pick_entries(weight_grad, pick_weight)
    kernel_vals = pick_entries(kernel_grad, pick_kernel)
    weight_sum, kernel_sum = lax.psum((weight_vals, kernel_vals), ("dp", "seq"))
    total_slots = local_utts * lax.axis_size("dp") * full_frames
    norm_factor = 1.0 / math.sqrt(total_slots)
    return (conv_out, context_grad, weight_sum * norm_factor, kernel_sum * norm_factor)


def solution(mesh):
    placed = (
        P("dp", "seq", None),
        P("dp", "seq", None),
        P("dp", "seq", None),
        P("dp", "seq", None),
        P("dp"),
        P(),
        P(),
        P("dp", "seq", None),
        P(),
        P(),
    )
    return jax.shard_map(
        on_device,
        mesh=mesh,
        in_specs=placed,
        out_specs=(P("dp", "seq", None), P("dp", "seq", None), P(), P()),
        check_vma=False,
    )
```

profile of v0, /device:TPU:1, one launch (start us, length us, event | category | flops | bytes accessed | tf_op | source)
XLA Modules:
  0.0 756.6 jit_solution(8033392045944065864)
XLA Ops:
  7.2 2.1 copy.22
  9.4 2.2 copy.23
  12.6 4.4 collective-permute-start.2
  28.5 3.3 fusion.104
  32.1 2.4 fusion.34
  34.5 99.7 %all-gather.3.cloned.1.call-done = bf16[2,2048,1536]{2,0,1:T(2,128)(2,1)} async-done(((bf16[2,64,1536]{2,0,1:T(2,128)(2,1)}), bf16[2,2048,1536]{2,0,1:T(2,128)(2,1)}) %all-gather.3.cloned.1.call-update) | async-done | bytes 12582928 | tf_op jit(solution)/shard_map/all_gather | solution.py:63
  134.2 31.1 %copy.24 = bf16[2,2048,1536]{1,2,0:T(8,128)(2,1)} copy(bf16[2,2048,1536]{2,0,1:T(2,128)(2,1)} %all-gather.3.cloned.1.call-done) | data formatting | bytes 25165824
  165.4 88.2 %all-gather.5.cloned.1.call-done = bf16[2,2048,1536]{2,0,1:T(2,128)(2,1)} async-done(((bf16[2,64,1536]{2,0,1:T(2,128)(2,1)}), bf16[2,2048,1536]{2,0,1:T(2,128)(2,1)}) %all-gather.5.cloned.1.call-update) | async-done | bytes 12582928 | tf_op jit(solution)/shard_map/all_gather | solution.py:62
  253.6 31.1 %copy.25 = bf16[2,2048,1536]{1,2,0:T(8,128)(2,1)} copy(bf16[2,2048,1536]{2,0,1:T(2,128)(2,1)} %all-gather.5.cloned.1.call-done) | data formatting | bytes 25165824
  284.7 51.8 %while.11 = (s32[]{:T(128)}, bf16[2,64,1536]{2,1,0:T(8,128)(2,1)S(1)}, bf16[2,2048,1536]{1,2,0:T(8,128)(2,1)}, s32[2]{0:T(128)S(1)}, bf16[2,64,1536]{2,1,0:T(8,1...) while((s32[]{:T(128)}, bf16[2,64,1536]{2,1,0:T(8,128)(2,1)S(1)}, ...), condition=%wide.region_3.4_spmd.clone, body=%wide.region_0.3_spmd.clone.sunk | while | flops 828571648 | bytes 65302632 | solution.py:83
  284.7 11.9 %constant_dynamic-slice_fusion.5 = (bf16[1,2048,1536]{1,2,0:T(8,128)(2,1)}, bf16[1,2048,1536]{1,2,0:T(8,128)(2,1)}) fusion(bf16[2,2048,1536]{1,2,0:T(8,128)(2,1)} %get-tuple-element.212, s32[]{:T(128)} %get-tuple-element.200, bf16[2,2048,1536]{1,2,0:T(8,128)(2,1)} %get-tuple-element.209), kind=kLoop, calls=%fused_computation.20.clone.1 | loop fusion | bytes 25165828 | tf_op jit(solution)/shard_map/while/body/jit(dynamic_index_in_dim)/dynamic_slice | solution.py:83
  298.2 5.0 fusion.182
  303.2 1.9 fusion.183
  305.1 5.1 fusion.184
  310.6 11.9 %constant_dynamic-slice_fusion.5 = (bf16[1,2048,1536]{1,2,0:T(8,128)(2,1)}, bf16[1,2048,1536]{1,2,0:T(8,128)(2,1)}) fusion(bf16[2,2048,1536]{1,2,0:T(8,128)(2,1)} %get-tuple-element.212, s32[]{:T(128)} %get-tuple-element.200, bf16[2,2048,1536]{1,2,0:T(8,128)(2,1)} %get-tuple-element.209), kind=kLoop, calls=%fused_computation.20.clone.1 | loop fusion | bytes 25165828 | tf_op jit(solution)/shard_map/while/body/jit(dynamic_index_in_dim)/dynamic_slice | solution.py:83
  324.1 5.0 fusion.182
  331.0 5.1 fusion.184
  336.6 5.0 convolution_bitcast_fusion
  342.4 10.5 %reshape_reshape.6 = f32[18432,128]{1,0:T(8,128)} reshape(f32[1536,1536]{1,0:T(8,128)} %convolution_bitcast_fusion) | data formatting | bytes 18874368 | tf_op jit(solution)/shard_map/reshape;reshape | solution.py:34
  353.0 48.0 %gather_fusion = f32[23592,128]{1,0:T(8,128)} fusion(f32[18432,128]{1,0:T(8,128)} %reshape_reshape.6, s32[24576]{0:T(1024)S(1)} %pad_clamp_fusion), kind=kCustom, calls=%fused_computation | custom fusion | bytes 24252576 | tf_op jit(solution)/shard_map/jit(_take)/gather | solution.py:35
  401.3 22.9 %select_reduce_fusion = f32[23592]{0:T(1024)} fusion(f32[23592,128]{1,0:T(8,128)} %gather_fusion, s32[23592]{0:T(1024)S(1)} %copy-done.2, pred[23592]{0:T(1024)(128)(4,1)S(1)} %copy-done.4), kind=kLoop, calls=%fused_computation.25 | loop fusion | flops 12055512 | bytes 12291432 | tf_op jit(solution)/shard_map/reduce_sum | solution.py:38
  427.0 235.6 %all-reduce.2.cloned.1.call-done = f32[23592]{0:T(1024)} async-done(((f32[23592]{0:T(1024)}), f32[23592]{0:T(1024)}) %all-reduce.2.cloned.1.call-update) | async-done | bytes 94384 | tf_op jit(solution)/shard_map/psum | solution.py:120
  670.6 74.1 %psum.15 = f32[476]{0:T(512)S(1)} all-reduce(f32[476]{0:T(512)S(1)} %select_reduce_fusion.1), channel_id=1, replica_groups=mesh['dp'=8,'seq'=32] {'dp','seq'}, use_global_device_ids=true, to_apply=%region_38.39 | all-reduce | flops 476 | bytes 3808 | tf_op jit(solution)/shard_map/psum | solution.py:120
  745.6 4.5 fusion.70
  (237 shorter events, 30.2 us)
Async XLA Ops:
  7.2 127.1 %all-gather.3.cloned.1.call-start = ((), (), s32[]{:S(2)}) async-start(), calls=%async_computation | async-start | bytes 12976128 | tf_op jit(solution)/shard_map/all_gather | solution.py:63
  9.4 244.2 %all-gather.5.cloned.1.call-start = ((), (), s32[]{:S(2)}) async-start(), calls=%async_computation.1 | async-start | bytes 12976128 | tf_op jit(solution)/shard_map/all_gather | solution.py:62
  11.6 650.9 %all-reduce.2.cloned.1.call-start = ((), (), s32[]{:S(2)}) async-start(), calls=%async_computation.2 | async-start | bytes 196608 | tf_op jit(solution)/shard_map/psum | solution.py:120
  12.6 14.5 %collective-permute-start.2 = (bf16[2,15,1536]{2,1,0:T(8,128)(2,1)S(1)}, bf16[2,15,1536]{2,1,0:T(8,128)(2,1)S(1)}, u32[]{:S(2)}, u32[]{:S(2)}) collective-permute-start(bf16[2,15,1536]{2,1,0:T(8,128)(2,1)S(1)} %get-tuple-element.144), channel_id=1, source_target_pairs={{0,1},{1,2},{2,3},{3,4},{4,5},{5,6},{6,7},{7,8},{8,9},{9,10},{10,1... | collective-permute-start | bytes 276488 | tf_op jit(solution)/shard_map/ppermute | solution.py:18
  17.0 10.1 %collective-permute-start.3 = (bf16[2,15,1536]{2,1,0:T(8,128)(2,1)S(1)}, bf16[2,15,1536]{2,1,0:T(8,128)(2,1)S(1)}, u32[]{:S(2)}, u32[]{:S(2)}) collective-permute-start(bf16[2,15,1536]{2,1,0:T(8,128)(2,1)S(1)} %get-tuple-element.145), channel_id=1, source_target_pairs={{1,0},{2,1},{3,2},{4,3},{5,4},{6,5},{7,6},{8,7},{9,8},{10,9},{11,1... | collective-permute-start | bytes 276488 | tf_op jit(solution)/shard_map/ppermute | solution.py:19
  401.0 344.3 %copy-start.6 = (f32[1536]{0:T(1024)S(1)}, f32[1536]{0:T(1024)}, u32[]{:S(2)}) copy-start(f32[1536]{0:T(1024)} %copy-done.5) | copy-start | bytes 18436
  401.0 344.3 %copy-start.8 = (f32[1536]{0:T(1024)S(1)}, f32[1536]{0:T(1024)}, u32[]{:S(2)}) copy-start(f32[1536]{0:T(1024)} %copy-done.7) | copy-start | bytes 18436
  401.0 344.3 %copy-start.10 = (f32[1536]{0:T(1024)S(1)}, f32[1536]{0:T(1024)}, u32[]{:S(2)}) copy-start(f32[1536]{0:T(1024)} %copy-done.9) | copy-start | bytes 18436
  401.0 344.3 %copy-start.12 = (f32[1536]{0:T(1024)S(1)}, f32[1536]{0:T(1024)}, u32[]{:S(2)}) copy-start(f32[1536]{0:T(1024)} %copy-done.11) | copy-start | bytes 18436
  401.0 344.3 %copy-start.14 = (f32[1536]{0:T(1024)S(1)}, f32[1536]{0:T(1024)}, u32[]{:S(2)}) copy-start(f32[1536]{0:T(1024)} %copy-done.13) | copy-start | bytes 18436
  401.0 344.3 %copy-start.16 = (f32[1536]{0:T(1024)S(1)}, f32[1536]{0:T(1024)}, u32[]{:S(2)}) copy-start(f32[1536]{0:T(1024)} %copy-done.15) | copy-start | bytes 18436
  401.0 344.3 %copy-start.18 = (f32[1536]{0:T(1024)S(1)}, f32[1536]{0:T(1024)}, u32[]{:S(2)}) copy-start(f32[1536]{0:T(1024)} %copy-done.17) | copy-start | bytes 18436
  401.0 344.3 %copy-start.20 = (f32[1536]{0:T(1024)S(1)}, f32[1536]{0:T(1024)}, u32[]{:S(2)}) copy-start(f32[1536]{0:T(1024)} %copy-done.19) | copy-start | bytes 18436
  401.1 344.3 %copy-start.22 = (f32[1536]{0:T(1024)S(1)}, f32[1536]{0:T(1024)}, u32[]{:S(2)}) copy-start(f32[1536]{0:T(1024)} %copy-done.21) | copy-start | bytes 18436
  401.1 344.3 %copy-start.24 = (f32[1536]{0:T(1024)S(1)}, f32[1536]{0:T(1024)}, u32[]{:S(2)}) copy-start(f32[1536]{0:T(1024)} %copy-done.23) | copy-start | bytes 18436
  401.1 344.3 %copy-start.26 = (f32[1536]{0:T(1024)S(1)}, f32[1536]{0:T(1024)}, u32[]{:S(2)}) copy-start(f32[1536]{0:T(1024)} %copy-done.25) | copy-start | bytes 18436
  401.1 344.3 %copy-start.28 = (f32[1536]{0:T(1024)S(1)}, f32[1536]{0:T(1024)}, u32[]{:S(2)}) copy-start(f32[1536]{0:T(1024)} %copy-done.27) | copy-start | bytes 18436
  401.1 344.3 %copy-start.30 = (f32[1536]{0:T(1024)S(1)}, f32[1536]{0:T(1024)}, u32[]{:S(2)}) copy-start(f32[1536]{0:T(1024)} %copy-done.29) | copy-start | bytes 18436
  401.1 344.3 %copy-start.32 = (f32[1536]{0:T(1024)S(1)}, f32[1536]{0:T(1024)}, u32[]{:S(2)}) copy-start(f32[1536]{0:T(1024)} %copy-done.31) | copy-start | bytes 18436
  401.1 344.3 %copy-start.34 = (f32[1536]{0:T(1024)S(1)}, f32[1536]{0:T(1024)}, u32[]{:S(2)}) copy-start(f32[1536]{0:T(1024)} %copy-done.33) | copy-start | bytes 18436
  401.1 344.3 %copy-start.36 = (f32[1536]{0:T(1024)S(1)}, f32[1536]{0:T(1024)}, u32[]{:S(2)}) copy-start(f32[1536]{0:T(1024)} %copy-done.35) | copy-start | bytes 18436
  401.1 344.3 %copy-start.38 = (f32[1536]{0:T(1024)S(1)}, f32[1536]{0:T(1024)}, u32[]{:S(2)}) copy-start(f32[1536]{0:T(1024)} %copy-done.37) | copy-start | bytes 18436
  424.3 239.8 %collective-permute-start = (bf16[2,15,1536]{2,1,0:T(8,128)(2,1)S(1)}, bf16[2,15,1536]{2,1,0:T(8,128)(2,1)S(1)}, u32[]{:S(2)}, u32[]{:S(2)}) collective-permute-start(bf16[2,15,1536]{2,1,0:T(8,128)(2,1)S(1)} %get-tuple-element.146), channel_id=1, source_target_pairs={{0,1},{1,2},{2,3},{3,4},{4,5},{5,6},{6,7},{7,8},{8,9},{9,10},{10,1... | collective-permute-start | bytes 276488 | tf_op jit(solution)/shard_map/ppermute | solution.py:18
  425.7 239.7 %collective-permute-start.1 = (bf16[2,15,1536]{2,1,0:T(8,128)(2,1)S(1)}, bf16[2,15,1536]{2,1,0:T(8,128)(2,1)S(1)}, u32[]{:S(2)}, u32[]{:S(2)}) collective-permute-start(bf16[2,15,1536]{2,1,0:T(8,128)(2,1)S(1)} %get-tuple-element.147), channel_id=1, source_target_pairs={{1,0},{2,1},{3,2},{4,3},{5,4},{6,5},{7,6},{8,7},{9,8},{10,9},{11,1... | collective-permute-start | bytes 276488 | tf_op jit(solution)/shard_map/ppermute | solution.py:19
  (58 other events, 6625.0 us)
Sparse Core Ops, SparseCore 0:
  11.2 123.0 all-gather.2
  136.8 116.7 all-gather.4
  424.3 238.1 all-reduce.1
where the time goes:
time: 759 us; the launch traced here: 757 us
  waiting for transfers between devices  424 us (56%)
  local copies, waits for them, and re-layouts  155 us (20%)
  blocking collectives  74.1 us (10%)
  other arithmetic  51.7 us (7%)
  matrix products  28.4 us (4%)
  between operations  15.2 us (2%)
  starting transfers between devices  8.5 us (1%)
    psum x1, waiting for transfers between devices, on_device(): weight_sum, kernel_sum = lax.psum((weight_vals, kernel_vals), ('dp', 'seq'))  236 us
    all_gather x1, waiting for transfers between devices, on_device(): lax.all_gather(value_rows, 'seq', axis=1, tiled=True)  99.7 us
    all_gather x1, waiting for transfers between devices, on_device(): lax.all_gather(key_rows, 'seq', axis=1, tiled=True)  88.2 us
    psum x1, blocking collectives, on_device(): weight_sum, kernel_sum = lax.psum((weight_vals, kernel_vals), ('dp', 'seq'))  74.1 us
    unnamed x154, local copies, waits for them, and re-layouts  66.9 us
    gather x2, local copies, waits for them, and re-layouts, pick_entries(): chosen = jnp.take(blocks, picks // lane, axis=0)  49.1 us
    dynamic_slice x6, local copies, waits for them, and re-layouts, on_device(): context = lax.map(one_utt, (queries, all_keys, all_values, utt_lengths))  25.1 us
    reduce_sum x2, other arithmetic, pick_entries(): return jnp.sum(jnp.where(hit, chosen, jnp.float32(0.0)), axis=1)  23.2 us
  transfers between devices with their start and end apart: 7, of which 3 were waited for; matrix products, arithmetic and copies ran while one was open for 7% of the time, Pallas kernels for 0%

commit v1 on v0

--- a/solution.py
+++ b/solution.py
@@ -117,7 +117,7 @@
     context_grad = context_grad.reshape(local_utts, frames_dev, width).astype(jnp.bfloat16)
     weight_vals = pick_entries(weight_grad, pick_weight)
     kernel_vals = pick_entries(kernel_grad, pick_kernel)
-    weight_sum, kernel_sum = lax.psum((weight_vals, kernel_vals), ("dp", "seq"))
+    weight_sum, kernel_sum = lax.psum(lax.psum((weight_vals, kernel_vals), "dp"), "seq")
     total_slots = local_utts * lax.axis_size("dp") * full_frames
     norm_factor = 1.0 / math.sqrt(total_slots)
     return (conv_out, context_grad, weight_sum * norm_factor, kernel_sum * norm_factor)

time: 759 us -> 644 us (0.85)
  waiting for transfers between devices: 424 us -> 299 us
    psum x1 -> x2, waiting for transfers between devices: 236 us -> 107 us  [the longest x1 54.1 us: on_device(): lax.psum((weight_vals, kernel_vals), 'dp')]
    psum x1 -> x2, blocking collectives: 74.1 us -> 75.5 us  [the longest x1 61 us: on_device(): lax.psum(lax.psum((weight_vals, kernel_vals), 'dp'), 'seq')]
    unnamed x154 -> x146, local copies, waits for them, and re-layouts: 66.9 us -> 66.8 us
  transfers between devices with their start and end apart: 7 -> 8, of which waited for: 3 -> 4; matrix products, arithmetic and copies ran while one was open for 7% -> 23% of each run, Pallas kernels for 0% -> 0%
where the time goes in v1:
time: 644 us; the launch traced here: 638 us
  waiting for transfers between devices  299 us (46%)
  local copies, waits for them, and re-layouts  155 us (24%)
  blocking collectives  75.5 us (12%)
  other arithmetic  51.3 us (8%)
  matrix products  33.1 us (5%)
  between operations  15.2 us (2%)
  starting transfers between devices  8.72 us (1%)
    all_gather x1, waiting for transfers between devices, on_device(): lax.all_gather(value_rows, 'seq', axis=1, tiled=True)  102 us
    all_gather x1, waiting for transfers between devices, on_device(): lax.all_gather(key_rows, 'seq', axis=1, tiled=True)  88.8 us
    unnamed x146, local copies, waits for them, and re-layouts  66.8 us
    psum x1, blocking collectives, on_device(): lax.psum(lax.psum((weight_vals, kernel_vals), 'dp'), 'seq')  61 us
    psum x1, waiting for transfers between devices, on_device(): lax.psum((weight_vals, kernel_vals), 'dp')  54.1 us
    psum x1, waiting for transfers between devices, on_device(): lax.psum(lax.psum((weight_vals, kernel_vals), 'dp'), 'seq')  53.3 us
    gather x2, local copies, waits for them, and re-layouts, pick_entries(): chosen = jnp.take(blocks, picks // lane, axis=0)  49.1 us
    dynamic_slice x6, local copies, waits for them, and re-layouts, on_device(): context = lax.map(one_utt, (queries, all_keys, all_values, utt_lengths))  25.1 us
  transfers between devices with their start and end apart: 8, of which 4 were waited for; matrix products, arithmetic and copies ran while one was open for 23% of the time, Pallas kernels for 0%

profile of v1, /device:TPU:1, one launch (start us, length us, event | category | flops | bytes accessed | tf_op | source)
XLA Modules:
  0.0 637.8 jit_solution(4167659140105766210)
XLA Ops:
  12.6 4.4 collective-permute-start.2
  28.3 3.1 fusion.104
  31.8 102.5 %all-gather.3.cloned.1.call-done = bf16[2,2048,1536]{2,0,1:T(2,128)(2,1)} async-done(((bf16[2,64,1536]{2,0,1:T(2,128)(2,1)}), bf16[2,2048,1536]{2,0,1:T(2,128)(2,1)}) %all-gather.3.cloned.1.call-update) | async-done | bytes 12582928 | tf_op jit(solution)/shard_map/all_gather | solution.py:63
  134.2 31.1 %copy.24 = bf16[2,2048,1536]{1,2,0:T(8,128)(2,1)} copy(bf16[2,2048,1536]{2,0,1:T(2,128)(2,1)} %all-gather.3.cloned.1.call-done) | data formatting | bytes 25165824
  165.3 88.8 %all-gather.5.cloned.1.call-done = bf16[2,2048,1536]{2,0,1:T(2,128)(2,1)} async-done(((bf16[2,64,1536]{2,0,1:T(2,128)(2,1)}), bf16[2,2048,1536]{2,0,1:T(2,128)(2,1)}) %all-gather.5.cloned.1.call-update) | async-done | bytes 12582928 | tf_op jit(solution)/shard_map/all_gather | solution.py:62
  254.2 31.1 %copy.25 = bf16[2,2048,1536]{1,2,0:T(8,128)(2,1)} copy(bf16[2,2048,1536]{2,0,1:T(2,128)(2,1)} %all-gather.5.cloned.1.call-done) | data formatting | bytes 25165824
  285.3 51.9 %while.11 = (s32[]{:T(128)}, bf16[2,64,1536]{2,1,0:T(8,128)(2,1)S(1)}, bf16[2,2048,1536]{1,2,0:T(8,128)(2,1)}, s32[2]{0:T(128)S(1)}, bf16[2,64,1536]{2,1,0:T(8,1...) while((s32[]{:T(128)}, bf16[2,64,1536]{2,1,0:T(8,128)(2,1)S(1)}, ...), condition=%wide.region_3.4_spmd.clone, body=%wide.region_0.3_spmd.clone.sunk | while | flops 828571648 | bytes 65302632 | solution.py:83
  285.3 12.0 %constant_dynamic-slice_fusion.5 = (bf16[1,2048,1536]{1,2,0:T(8,128)(2,1)}, bf16[1,2048,1536]{1,2,0:T(8,128)(2,1)}) fusion(bf16[2,2048,1536]{1,2,0:T(8,128)(2,1)} %get-tuple-element.212, s32[]{:T(128)} %get-tuple-element.200, bf16[2,2048,1536]{1,2,0:T(8,128)(2,1)} %get-tuple-element.209), kind=kLoop, calls=%fused_computation.20.clone.1 | loop fusion | bytes 25165828 | tf_op jit(solution)/shard_map/while/body/jit(dynamic_index_in_dim)/dynamic_slice | solution.py:83
  298.8 5.0 fusion.182
  305.7 5.1 fusion.184
  311.3 11.9 %constant_dynamic-slice_fusion.5 = (bf16[1,2048,1536]{1,2,0:T(8,128)(2,1)}, bf16[1,2048,1536]{1,2,0:T(8,128)(2,1)}) fusion(bf16[2,2048,1536]{1,2,0:T(8,128)(2,1)} %get-tuple-element.212, s32[]{:T(128)} %get-tuple-element.200, bf16[2,2048,1536]{1,2,0:T(8,128)(2,1)} %get-tuple-element.209), kind=kLoop, calls=%fused_computation.20.clone.1 | loop fusion | bytes 25165828 | tf_op jit(solution)/shard_map/while/body/jit(dynamic_index_in_dim)/dynamic_slice | solution.py:83
  324.7 5.0 fusion.182
  331.6 5.1 fusion.184
  337.2 3.2 fusion.37
  342.0 5.0 convolution_bitcast_fusion
  347.1 10.5 %reshape_reshape.6 = f32[18432,128]{1,0:T(8,128)} reshape(f32[1536,1536]{1,0:T(8,128)} %convolution_bitcast_fusion) | data formatting | bytes 18874368 | tf_op jit(solution)/shard_map/reshape;reshape | solution.py:34
  357.6 48.0 %gather_fusion = f32[23592,128]{1,0:T(8,128)} fusion(f32[18432,128]{1,0:T(8,128)} %reshape_reshape.6, s32[24576]{0:T(1024)S(1)} %pad_clamp_fusion), kind=kCustom, calls=%fused_computation | custom fusion | bytes 24252576 | tf_op jit(solution)/shard_map/jit(_take)/gather | solution.py:35
  405.5 22.9 %select_reduce_fusion = f32[23592]{0:T(1024)} fusion(f32[23592,128]{1,0:T(8,128)} %gather_fusion, s32[23592]{0:T(1024)S(1)} %copy-done.2, pred[23592]{0:T(1024)(128)(4,1)S(1)} %copy-done.4), kind=kLoop, calls=%fused_computation.25 | loop fusion | flops 12055512 | bytes 12291432 | tf_op jit(solution)/shard_map/reduce_sum | solution.py:38
  428.8 4.7 fusion.34
  434.8 54.1 %all-reduce.3.cloned.1.call-done = f32[23592]{0:T(1024)} async-done(((f32[23592]{0:T(1024)}), f32[23592]{0:T(1024)}) %all-reduce.3.cloned.1.call-update) | async-done | bytes 94384 | tf_op jit(solution)/shard_map/psum | solution.py:120
  495.5 14.5 %psum.30 = f32[476]{0:T(512)S(1)} all-reduce(f32[476]{0:T(512)S(1)} %select_reduce_fusion.1), channel_id=1, replica_groups=mesh['dp'=8,'seq'=32] {'dp'}, use_global_device_ids=true, to_apply=%region_39.40 | all-reduce | flops 476 | bytes 3808 | tf_op jit(solution)/shard_map/psum | solution.py:120
  510.0 61.0 %psum.31 = f32[476]{0:T(512)S(1)} all-reduce(f32[476]{0:T(512)S(1)} %psum.30), channel_id=1, replica_groups=mesh['dp'=8,'seq'=32] {'seq'}, use_global_device_ids=true, to_apply=%region_40.41 | all-reduce | flops 476 | bytes 3808 | tf_op jit(solution)/shard_map/psum | solution.py:120
  571.3 4.5 fusion.70
  576.4 53.3 %all-reduce.5.cloned.1.call-done = f32[23592]{0:T(1024)} async-done(((f32[23592]{0:T(1024)}), f32[23592]{0:T(1024)}) %all-reduce.5.cloned.1.call-update) | async-done | bytes 94384 | tf_op jit(solution)/shard_map/psum | solution.py:120
  (231 shorter events, 35.6 us)
Async XLA Ops:
  7.2 127.1 %all-gather.3.cloned.1.call-start = ((), (), s32[]{:S(2)}) async-start(), calls=%async_computation | async-start | bytes 12976128 | tf_op jit(solution)/shard_map/all_gather | solution.py:63
  9.4 244.8 %all-gather.5.cloned.1.call-start = ((), (), s32[]{:S(2)}) async-start(), calls=%async_computation.1 | async-start | bytes 12976128 | tf_op jit(solution)/shard_map/all_gather | solution.py:62
  11.6 477.3 %all-reduce.3.cloned.1.call-start = ((), (), s32[]{:S(2)}) async-start(), calls=%async_computation.2 | async-start | bytes 196608 | tf_op jit(solution)/shard_map/psum | solution.py:120
  12.6 14.5 %collective-permute-start.2 = (bf16[2,15,1536]{2,1,0:T(8,128)(2,1)S(1)}, bf16[2,15,1536]{2,1,0:T(8,128)(2,1)S(1)}, u32[]{:S(2)}, u32[]{:S(2)}) collective-permute-start(bf16[2,15,1536]{2,1,0:T(8,128)(2,1)S(1)} %get-tuple-element.144), channel_id=1, source_target_pairs={{0,1},{1,2},{2,3},{3,4},{4,5},{5,6},{6,7},{7,8},{8,9},{9,10},{10,1... | collective-permute-start | bytes 276488 | tf_op jit(solution)/shard_map/ppermute | solution.py:18
  17.0 10.1 %collective-permute-start.3 = (bf16[2,15,1536]{2,1,0:T(8,128)(2,1)S(1)}, bf16[2,15,1536]{2,1,0:T(8,128)(2,1)S(1)}, u32[]{:S(2)}, u32[]{:S(2)}) collective-permute-start(bf16[2,15,1536]{2,1,0:T(8,128)(2,1)S(1)} %get-tuple-element.145), channel_id=1, source_target_pairs={{1,0},{2,1},{3,2},{4,3},{5,4},{6,5},{7,6},{8,7},{9,8},{10,9},{11,1... | collective-permute-start | bytes 276488 | tf_op jit(solution)/shard_map/ppermute | solution.py:19
  340.4 148.5 %collective-permute-start = (bf16[2,15,1536]{2,1,0:T(8,128)(2,1)S(1)}, bf16[2,15,1536]{2,1,0:T(8,128)(2,1)S(1)}, u32[]{:S(2)}, u32[]{:S(2)}) collective-permute-start(bf16[2,15,1536]{2,1,0:T(8,128)(2,1)S(1)} %get-tuple-element.146), channel_id=1, source_target_pairs={{0,1},{1,2},{2,3},{3,4},{4,5},{5,6},{6,7},{7,8},{8,9},{9,10},{10,1... | collective-permute-start | bytes 276488 | tf_op jit(solution)/shard_map/ppermute | solution.py:18
  428.4 142.6 %copy-start.6 = (f32[1536]{0:T(1024)S(1)}, f32[1536]{0:T(1024)}, u32[]{:S(2)}) copy-start(f32[1536]{0:T(1024)} %copy-done.5) | copy-start | bytes 18436
  428.4 142.6 %copy-start.8 = (f32[1536]{0:T(1024)S(1)}, f32[1536]{0:T(1024)}, u32[]{:S(2)}) copy-start(f32[1536]{0:T(1024)} %copy-done.7) | copy-start | bytes 18436
  428.5 142.6 %copy-start.10 = (f32[1536]{0:T(1024)S(1)}, f32[1536]{0:T(1024)}, u32[]{:S(2)}) copy-start(f32[1536]{0:T(1024)} %copy-done.9) | copy-start | bytes 18436
  428.5 142.6 %copy-start.12 = (f32[1536]{0:T(1024)S(1)}, f32[1536]{0:T(1024)}, u32[]{:S(2)}) copy-start(f32[1536]{0:T(1024)} %copy-done.11) | copy-start | bytes 18436
  428.5 142.6 %copy-start.14 = (f32[1536]{0:T(1024)S(1)}, f32[1536]{0:T(1024)}, u32[]{:S(2)}) copy-start(f32[1536]{0:T(1024)} %copy-done.13) | copy-start | bytes 18436
  428.5 142.6 %copy-start.16 = (f32[1536]{0:T(1024)S(1)}, f32[1536]{0:T(1024)}, u32[]{:S(2)}) copy-start(f32[1536]{0:T(1024)} %copy-done.15) | copy-start | bytes 18436
  428.5 142.6 %copy-start.18 = (f32[1536]{0:T(1024)S(1)}, f32[1536]{0:T(1024)}, u32[]{:S(2)}) copy-start(f32[1536]{0:T(1024)} %copy-done.17) | copy-start | bytes 18436
  428.5 142.6 %copy-start.20 = (f32[1536]{0:T(1024)S(1)}, f32[1536]{0:T(1024)}, u32[]{:S(2)}) copy-start(f32[1536]{0:T(1024)} %copy-done.19) | copy-start | bytes 18436
  428.5 142.6 %copy-start.22 = (f32[1536]{0:T(1024)S(1)}, f32[1536]{0:T(1024)}, u32[]{:S(2)}) copy-start(f32[1536]{0:T(1024)} %copy-done.21) | copy-start | bytes 18436
  428.5 142.6 %copy-start.24 = (f32[1536]{0:T(1024)S(1)}, f32[1536]{0:T(1024)}, u32[]{:S(2)}) copy-start(f32[1536]{0:T(1024)} %copy-done.23) | copy-start | bytes 18436
  428.5 142.6 %copy-start.26 = (f32[1536]{0:T(1024)S(1)}, f32[1536]{0:T(1024)}, u32[]{:S(2)}) copy-start(f32[1536]{0:T(1024)} %copy-done.25) | copy-start | bytes 18436
  428.5 142.6 %copy-start.28 = (f32[1536]{0:T(1024)S(1)}, f32[1536]{0:T(1024)}, u32[]{:S(2)}) copy-start(f32[1536]{0:T(1024)} %copy-done.27) | copy-start | bytes 18436
  428.6 142.6 %copy-start.30 = (f32[1536]{0:T(1024)S(1)}, f32[1536]{0:T(1024)}, u32[]{:S(2)}) copy-start(f32[1536]{0:T(1024)} %copy-done.29) | copy-start | bytes 18436
  428.6 142.6 %copy-start.32 = (f32[1536]{0:T(1024)S(1)}, f32[1536]{0:T(1024)}, u32[]{:S(2)}) copy-start(f32[1536]{0:T(1024)} %copy-done.31) | copy-start | bytes 18436
  428.6 142.6 %copy-start.34 = (f32[1536]{0:T(1024)S(1)}, f32[1536]{0:T(1024)}, u32[]{:S(2)}) copy-start(f32[1536]{0:T(1024)} %copy-done.33) | copy-start | bytes 18436
  428.6 142.6 %copy-start.36 = (f32[1536]{0:T(1024)S(1)}, f32[1536]{0:T(1024)}, u32[]{:S(2)}) copy-start(f32[1536]{0:T(1024)} %copy-done.35) | copy-start | bytes 18436
  428.8 200.9 %all-reduce.5.cloned.1.call-start = ((), (), s32[]{:S(2)}) async-start(), calls=%async_computation.3 | async-start | bytes 196608 | tf_op jit(solution)/shard_map/psum | solution.py:120
  433.5 56.7 %collective-permute-start.1 = (bf16[2,15,1536]{2,1,0:T(8,128)(2,1)S(1)}, bf16[2,15,1536]{2,1,0:T(8,128)(2,1)S(1)}, u32[]{:S(2)}, u32[]{:S(2)}) collective-permute-start(bf16[2,15,1536]{2,1,0:T(8,128)(2,1)S(1)} %get-tuple-element.147), channel_id=1, source_target_pairs={{1,0},{2,1},{3,2},{4,3},{5,4},{6,5},{7,6},{8,7},{9,8},{10,9},{11,1... | collective-permute-start | bytes 276488 | tf_op jit(solution)/shard_map/ppermute | solution.py:19
  (55 other events, 3174.1 us)
Sparse Core Ops, SparseCore 0:
  11.2 123.0 all-gather.2
  137.4 116.7 all-gather.4
  428.9 59.9 all-reduce.2
  492.6 137.0 all-reduce.4
